TPU v7x, 32 devices: a whole 2x2x4 slice. The times are simulated.
32 devices in a mesh: groups: 2 (over y), tensor: 8 (over z, x), dp: 2 (over core).
Axes of the slice: x: 2, y: 2, z: 4, core: 2. Of those that a mesh axis runs over, the one named last changes fastest.
Arguments:
- hidden: bfloat16 [2400, 8192], P(('groups', 'dp'), 'tensor'), parts along dimension 0, may hold values from -6 to 6
- norm_gain: float32 [8192], replicated, may hold values from 0.1 to 1.9
- query_weight: bfloat16 [8192, 8192], P('dp', 'tensor'), may hold values from -0.09375 to 0.09375
- query_keep: int32 [128, 128], P('dp', 'tensor'), may hold values 0 or 1
- kv_weight: bfloat16 [2048, 8192], P('tensor', 'dp'), may hold values from -0.0625 to 0.0625
- out_weight: bfloat16 [8192, 8192], P('tensor', 'dp'), may hold values from -0.5 to 0.5
- out_keep: int32 [128, 128], P('tensor', 'dp'), may hold values 0 or 1
- pair_lengths: int32 [4, 4], P(('groups', 'dp')), parts along dimension 0, may hold values from 1 to 300, 600 in all within a row
- premise_lengths: int32 [4, 4], P(('groups', 'dp')), parts along dimension 0, may hold values from 1 to 299
Outputs:
- attn_out: bfloat16 [2400, 8192], P(('groups', 'dp'), 'tensor'), parts along dimension 0
There are 2 independent parts, one for each index of `groups`. A program takes and returns all parts, laid end to end along the dimension named above; an argument that names none is the same for every part. Nothing has to cross between parts.
Inputs may be any that keep to these rules, and one draw needn't show every extreme that they name: `pair_lengths`: each row lists the 4 pair lengths of one batch in order; they sum to 600.
All inputs are finite; a program needn't handle non-finite values. No bound on the sum of `query_keep` or of `out_keep` on one device may be relied on, other than what follows from the above.
Results may differ from a plain program's by a relative error of at most 0.01.
Values may be sent and summed in bfloat16 or wider, within the bound.
No kernel may reach another device: no remote copies, remote signals or barrier semaphores. Data moves between devices by JAX's collectives and lax.ppermute only.
A program may use at most 192 MiB of HBM per device.

v0:
```python
import jax
import jax.numpy as jnp
from jax import lax
from jax.sharding import PartitionSpec as P

HEADS = 64
KVH = 8
HD = 128


def rotate_pairs(values, positions):
    half_width = values.shape[-1] // 2
    inverse = 500000.0 ** (-(jnp.arange(half_width, dtype=jnp.float32) * 2.0 / values.shape[-1]))
    angles = positions[:, None] * inverse[None, :]
    cosine = jnp.cos(angles)[:, None, :]
    sine_part = jnp.sin(angles)[:, None, :]
    first_half = values[..., :half_width]
    second_half = values[..., half_width:]
    return jnp.concatenate(
        [
            first_half * cosine - second_half * sine_part,
            second_half * cosine + first_half * sine_part,
        ],
        axis=-1,
    )


def pair_layout(lengths, premise, count):
    pair_ends = jnp.cumsum(lengths)
    pair_starts = pair_ends - lengths
    position = jnp.arange(count, dtype=jnp.int32)
    pair_index = jnp.sum((position[:, None] >= pair_ends[None, :]).astype(jnp.int32), axis=1)
    one_hot = (
        pair_index[:, None] == jnp.arange(lengths.shape[0], dtype=jnp.int32)[None, :]
    ).astype(jnp.int32)
    offset = position - jnp.sum(one_hot * pair_starts[None, :], axis=1)
    premise_used = jnp.minimum(premise, lengths - 1)
    in_premise = offset < jnp.sum(one_hot * premise_used[None, :], axis=1)
    allowed = (pair_index[:, None] == pair_index[None, :]) & (
        in_premise[None, :] | jnp.logical_not(in_premise)[:, None]
    )
    return (offset.astype(jnp.float32), allowed)


def prune(weight, keep):
    blocks = weight.reshape(
        keep.shape[0],
        weight.shape[0] // keep.shape[0],
        keep.shape[1],
        weight.shape[1] // keep.shape[1],
    )
    blocks = blocks * keep.astype(weight.dtype)[:, None, :, None]
    return blocks.reshape(weight.shape)


def on_device(
    hidden,
    norm_gain,
    query_weight,
    query_keep,
    kv_weight,
    out_weight,
    out_keep,
    pair_lengths,
    premise_lengths,
):
    tensor_rank = lax.axis_index("tensor")
    total_rows = hidden.shape[0]
    head_local = query_weight.shape[1] // HD
    query_pruned = prune(query_weight, query_keep)
    out_pruned = prune(out_weight, out_keep)
    query_full = lax.all_gather(query_pruned, "dp", axis=0, tiled=True)
    kv_full, out_full = (
        lax.all_gather(kv_weight, "dp", axis=1, tiled=True),
        lax.all_gather(out_pruned, "dp", axis=1, tiled=True),
    )
    whole = lax.all_gather(hidden, "tensor", axis=1, tiled=True)
    rows_float = whole.astype(jnp.float32)
    mean_square = jnp.mean(rows_float * rows_float, axis=-1, keepdims=True)
    normed = (rows_float * lax.rsqrt(mean_square + 1e-05) * norm_gain).astype(jnp.bfloat16)
    queries_raw = jnp.dot(normed, query_full, preferred_element_type=jnp.float32)
    kv_piece = lax.dot_general(
        normed, kv_full, (((1,), (1,)), ((), ())), preferred_element_type=jnp.float32
    ).astype(jnp.bfloat16)
    kv_whole = lax.all_gather(kv_piece, "tensor", axis=1, tiled=True)
    offsets, allowed = pair_layout(pair_lengths[0], premise_lengths[0], total_rows)
    queries = rotate_pairs(queries_raw.reshape(total_rows, head_local, HD), offsets).astype(
        jnp.bfloat16
    )
    keys_all = rotate_pairs(
        kv_whole[:, : KVH * HD].reshape(total_rows, KVH, HD).astype(jnp.float32), offsets
    ).astype(jnp.bfloat16)
    values_all = kv_whole[:, KVH * HD :].reshape(total_rows, KVH, HD)
    chosen = (tensor_rank * head_local + jnp.arange(head_local, dtype=jnp.int32)) // (HEADS // KVH)
    keys_used = jnp.take(keys_all, chosen, axis=1)
    values_used = jnp.take(values_all, chosen, axis=1)
    count_blocks = total_rows // total_rows
    scale = HD ** (-0.5)

    def attend(operands):
        query_block, allowed_block = operands
        scores = (
            jnp.einsum("qhd,khd->hqk", query_block, keys_used, preferred_element_type=jnp.float32)
            * scale
        )
        weighted = jnp.where(allowed_block[None, :, :], jnp.exp(scores), 0.0)
        probs = (weighted / jnp.sum(weighted, axis=-1, keepdims=True)).astype(jnp.bfloat16)
        return jnp.einsum(
            "hqk,khd->qhd", probs, values_used, preferred_element_type=jnp.float32
        ).astype(jnp.bfloat16)

    context = lax.map(
        attend,
        (
            queries.reshape(count_blocks, total_rows, head_local, HD),
            allowed.reshape(count_blocks, total_rows, total_rows),
        ),
    )
    context = context.reshape(total_rows, head_local * HD)
    terms = jnp.dot(context, out_full, preferred_element_type=jnp.float32)
    mixed = lax.psum_scatter(terms, "tensor", scatter_dimension=1, tiled=True)
    return mixed.astype(jnp.bfloat16)


def solution(mesh):
    placed = (
        P(("groups", "dp"), "tensor"),
        P(),
        P("dp", "tensor"),
        P("dp", "tensor"),
        P("tensor", "dp"),
        P("tensor", "dp"),
        P("tensor", "dp"),
        P(("groups", "dp"), None),
        P(("groups", "dp"), None),
    )
    return jax.shard_map(
        on_device,
        mesh=mesh,
        in_specs=placed,
        out_specs=P(("groups", "dp"), "tensor"),
        check_vma=False,
    )
```

profile of v0, /device:TPU:0, one launch (start us, length us, event | category | flops | bytes accessed | tf_op | source)
XLA Modules:
  0.0 643.1 jit_solution(441192260038344043)
XLA Ops:
  6.5 0.0 copy-start.1
  6.5 0.0 all-gather.6.cloned.1.call-start
  6.5 0.7 all-gather.6.cloned.1.call-update
  7.3 0.0 all-gather.8.cloned.1.call-start
  7.3 0.7 all-gather.8.cloned.1.call-update
  8.0 0.0 all-gather.12.cloned.1.call-start
  8.1 0.0 copy-done.1
  8.1 0.1 copy.25
  8.2 6.2 mul.162
  14.4 22.8 %mul.163 = bf16[4096,1024]{1,0:T(8,128)(2,1)} reshape(bf16[64,64,16,64]{3,2,1,0:T(8,128)(2,1)} %mul.162) | data formatting | bytes 16777216 | tf_op jit(solution)/shard_map/mul | solution.py:52
  37.2 10.7 %mul.164 = bf16[4096,1024]{1,0:T(8,128)(2,1)} multiply(bf16[4096,1024]{1,0:T(8,128)(2,1)} %param.13, bf16[4096,1024]{1,0:T(8,128)(2,1)} %mul.163) | non-fusion elementwise | flops 4194304 | bytes 25165824 | tf_op jit(solution)/shard_map/mul | solution.py:52
  47.9 0.0 all-gather.12.cloned.1.call-update
  47.9 0.0 copy-start.5
  47.9 0.0 all-gather.10.cloned.1.call-start
  48.0 106.5 %all-gather.6.cloned.1.call-done = bf16[600,8192]{1,0:T(8,128)(2,1)} async-done(((bf16[600,1024]{1,0:T(8,128)(2,1)}), bf16[600,8192]{1,0:T(8,128)(2,1)}) %all-gather.6.cloned.1.call-update) | async-done | bytes 9830416 | tf_op jit(solution)/shard_map/all_gather | solution.py:77
  154.5 5.8 fusion
  160.3 0.0 copy-start.2
  160.3 7.7 %all-gather.8.cloned.1.call-done = bf16[256,8192]{1,0:T(8,128)(2,1)} async-done(((bf16[256,4096]{1,0:T(8,128)(2,1)}), bf16[256,8192]{1,0:T(8,128)(2,1)}) %all-gather.8.cloned.1.call-update) | async-done | bytes 4194320 | tf_op jit(solution)/shard_map/all_gather | solution.py:74
  168.0 0.0 copy-done.5
  168.0 8.6 %fusion.27 = bf16[600,256]{1,0:T(8,128)(2,1)} fusion(bf16[256,8192]{1,0:T(8,128)(2,1)} %all-gather.8.cloned.1.call-done, bf16[600,8192]{1,0:T(8,128)(2,1)} %all-gather.6.cloned.1.call-done, f32[8192]{0:T(1024)S(1)} %copy-done.5, f32[600]{0:T(1024)S(1)} %add_rsqrt_fusion), kind=kOutput, calls=%fused_computation.38 | convolution fusion | flops 2536396800 | bytes 14367072 | tf_op jit(solution)/shard_map/dot_general | solution.py:82
  176.6 0.0 all-gather.10.cloned.1.call-update
  176.6 0.0 all-gather.14.cloned.1.call-start
  176.7 0.0 copy-done.2
  176.7 10.6 %mul.179 = bf16[16,64,64,64]{3,2,1,0:T(8,128)(2,1)} broadcast(bf16[16,64]{1,0:T(8,128)(2,1)S(1)} %convert_element_type.59), dimensions={0,2} | broadcast | bytes 8390656 | tf_op jit(solution)/shard_map/mul | solution.py:52
  187.3 23.1 %mul.180 = bf16[1024,4096]{1,0:T(8,128)(2,1)} reshape(bf16[16,64,64,64]{3,2,1,0:T(8,128)(2,1)} %mul.179) | data formatting | bytes 16777216 | tf_op jit(solution)/shard_map/mul | solution.py:52
  210.4 10.3 %mul.181 = bf16[1024,4096]{1,0:T(8,128)(2,1)} multiply(bf16[1024,4096]{1,0:T(8,128)(2,1)} %param.16, bf16[1024,4096]{1,0:T(8,128)(2,1)} %mul.180) | non-fusion elementwise | flops 4194304 | bytes 25165824 | tf_op jit(solution)/shard_map/mul | solution.py:52
  220.7 0.0 copy-start.3
  220.7 0.0 copy-start.4
  220.7 0.0 all-gather.14.cloned.1.call-update
  220.8 0.2 reduce-scatter.2.cloned.1.call-start
  221.0 0.4 copy-done.3
  221.4 0.2 reduce-window.4
  221.6 0.1 convert_reduce_fusion
  221.7 0.0 copy-done.4
  221.7 0.1 select_reduce_fusion
  221.9 0.4 or_and_fusion
  222.2 1.1 multiply_cosine_fusion
  223.4 0.0 all-gather.12.cloned.1.call-done
  223.4 15.6 %fusion.9 = f32[75,8,8,128]{3,1,2,0:T(8,128)S(1)} fusion(bf16[8192,1024]{1,0:T(8,128)(2,1)} %all-gather.12.cloned.1.call-done, bf16[600,8192]{1,0:T(8,128)(2,1)} %all-gather.6.cloned.1.call-done, f32[8192]{0:T(1024)S(1)} %copy-done.5, f32[600]{0:T(1024)S(1)} %add_rsqrt_fusion), kind=kOutput, calls=%fused_computation.18 | convolution fusion | flops 10085990400 | bytes 29100384 | tf_op jit(solution)/shard_map/dot_general | solution.py:81
  239.0 0.6 copy.39
  239.6 19.9 %all-gather.10.cloned.1.call-done = bf16[600,2048]{1,0:T(8,128)(2,1)} async-done(((bf16[600,256]{1,0:T(8,128)(2,1)}), bf16[600,2048]{1,0:T(8,128)(2,1)}) %all-gather.10.cloned.1.call-update) | async-done | bytes 2457616 | tf_op jit(solution)/shard_map/all_gather | solution.py:85
  259.4 2.1 slice_bitcast_fusion
  261.5 0.6 copy.40
  262.1 1.3 copy.54
  263.4 1.9 fusion.42
  265.3 2.9 subtract_convert_fusion
  268.1 0.0 copy-start
  268.1 0.7 pad_maximum_fusion
  268.8 1.7 gather_fusion.1
  270.5 0.0 copy-done
  270.5 0.8 gather_fusion
  271.3 6.8 %fusion.3 = (f32[8,600]{1,0:T(8,128)S(1)}, f32[8,600,600]{1,2,0:T(8,128)S(1)}) fusion(pred[600,600]{0,1:T(8,128)(4,1)S(1)} %or_and_fusion, bf16[8,600,128]{2,1,0:T(8,128)(2,1)} %gather_fusion.1, pred[8]{0:T(512)(128)(4,1)S(1)} %compare_and_fusion, bf16[600,8,64]{2,0,1:T(8,128)(2,1)} %get-tuple-element.38, bf16[600,8,64]{2,0,1:T(8,128)(2,1)} %get-tuple-element.39), kind=kOutput, calls=%fused_computation.9 | convolution fusion | flops 748987200 | bytes 14356808 | tf_op jit(solution)/shard_map/while/body/eval_jaxpr/qhd,khd->hqk/dot_general | solution.py:103
  278.1 4.4 fusion.13
  282.6 6.6 %all-gather.14.cloned.1.call-done = bf16[1024,8192]{1,0:T(8,128)(2,1)} async-done(((bf16[1024,4096]{1,0:T(8,128)(2,1)}), bf16[1024,8192]{1,0:T(8,128)(2,1)}) %all-gather.14.cloned.1.call-update) | async-done | bytes 16777232 | tf_op jit(solution)/shard_map/all_gather | solution.py:75
  289.2 17.6 %fusion.14 = f32[600,8192]{1,0:T(8,128)} fusion(bf16[1024,8192]{1,0:T(8,128)(2,1)} %all-gather.14.cloned.1.call-done, bf16[8,75,8,128]{3,2,1,0:T(8,128)(2,1)S(1)} %fusion.13), kind=kOutput, calls=%fused_computation.22 | convolution fusion | flops 10066329600 | bytes 37666816 | tf_op jit(solution)/shard_map/dot_general | solution.py:120
  306.8 0.0 reduce-scatter.2.cloned.1.call-update
  306.8 326.6 %reduce-scatter.2.cloned.1.call-done = f32[600,1024]{1,0:T(8,128)} async-done(((f32[600,8192]{1,0:T(8,128)}), f32[600,1024]{1,0:T(8,128)}) %reduce-scatter.2.cloned.1.call-update) | async-done | bytes 2457616 | tf_op jit(solution)/shard_map/reduce_scatter | solution.py:121
  633.4 2.9 convert_element_type.60
  (10 shorter events, 0.1 us)
Async XLA Ops:
  6.5 1.5 copy-start.1
  6.5 148.0 %all-gather.6.cloned.1.call-start = ((), (), s32[]{:S(2)}) async-start(), calls=%async_computation.1 | async-start | bytes 11059200 | tf_op jit(solution)/shard_map/all_gather | solution.py:77
  7.3 160.7 %all-gather.8.cloned.1.call-start = ((), (), s32[]{:S(2)}) async-start(), calls=%async_computation.2 | async-start | bytes 6291456 | tf_op jit(solution)/shard_map/all_gather | solution.py:74
  8.0 215.4 %all-gather.12.cloned.1.call-start = ((), (), s32[]{:S(2)}) async-start(), calls=%async_computation.4 | async-start | bytes 25165824 | tf_op jit(solution)/shard_map/all_gather | solution.py:72
  47.9 120.1 %copy-start.5 = (f32[8192]{0:T(1024)S(1)}, f32[8192]{0:T(1024)}, u32[]{:S(2)}) copy-start(f32[8192]{0:T(1024)} %param.12) | copy-start | bytes 98308
  47.9 211.5 %all-gather.10.cloned.1.call-start = ((), (), s32[]{:S(2)}) async-start(), calls=%async_computation.3 | async-start | bytes 2764800 | tf_op jit(solution)/shard_map/all_gather | solution.py:85
  160.3 16.4 %copy-start.2 = (s32[16,64]{1,0:T(8,128)S(1)}, s32[16,64]{1,0:T(8,128)}, u32[]{:S(2)}) copy-start(s32[16,64]{1,0:T(8,128)} %param.17) | copy-start | bytes 12292
  176.6 112.5 %all-gather.14.cloned.1.call-start = ((), (), s32[]{:S(2)}) async-start(), calls=%async_computation.5 | async-start | bytes 25165824 | tf_op jit(solution)/shard_map/all_gather | solution.py:75
  220.7 0.7 copy-start.3
  220.7 1.0 copy-start.4
  220.8 412.6 %reduce-scatter.2.cloned.1.call-start = ((), (), s32[]{:S(2)}) async-start(), calls=%async_computation.6 | async-start | bytes 22118400 | tf_op jit(solution)/shard_map/reduce_scatter | solution.py:121
  268.1 2.4 copy-start
Sparse Core Ops, SparseCore 0:
  9.5 144.9 all-gather.5
  156.0 11.8 all-gather.7
  169.5 31.1 all-gather.11
  202.6 56.7 all-gather.9
  260.8 28.2 all-gather.13
  306.9 326.4 reduce-scatter.1
where the time goes:
time: 644 us; the launch traced here: 643 us
  waiting for transfers between devices  469 us (73%)
  local copies, waits for them, and re-layouts  70 us (11%)
  matrix products  53 us (8%)
  other arithmetic  37.3 us (6%)
  between operations  13.7 us (2%)
    reduce_scatter x1, waiting for transfers between devices, on_device(): mixed = lax.psum_scatter(terms, 'tensor', scatter_dimension=1, tiled=True)  327 us
    all_gather x1, waiting for transfers between devices, on_device(): whole = lax.all_gather(hidden, 'tensor', axis=1, tiled=True)  107 us
    mul x4, local copies, waits for them, and re-layouts, prune(): blocks = blocks * keep.astype(weight.dtype)[:, None, :, None]  62.7 us
    mul x2, other arithmetic, prune(): blocks = blocks * keep.astype(weight.dtype)[:, None, :, None]  21 us
    all_gather x1, waiting for transfers between devices, on_device(): kv_whole = lax.all_gather(kv_piece, 'tensor', axis=1, tiled=True)  19.9 us
    dot_general x1, matrix products, on_device(): terms = jnp.dot(context, out_full, preferred_element_type=jnp.float32)  17.6 us
    dot_general x1, matrix products, on_device(): jnp.dot(normed, query_full, preferred_element_type=jnp.float32)  15.6 us
  transfers between devices with their start and end apart: 6, of which 5 were waited for; matrix products, arithmetic and copies ran while one was open for 22% of the time, Pallas kernels for 0%

commit v1 on v0

--- a/solution.py
+++ b/solution.py
@@ -64,6 +64,18 @@
     pair_lengths,
     premise_lengths,
 ):
+
+    def _choose_tracks(xs, device_axis, axis_no):
+        y1, newest = (lax.axis_size(device_axis), lax.axis_index(device_axis))
+        out_arr, next_value = (xs, 1)
+        while next_value < y1:
+            u1 = lax.ppermute(out_arr, device_axis, [(at, at ^ next_value) for at in range(y1)])
+            x_next = jnp.concatenate([out_arr, u1], axis_no)
+            taken_in = jnp.concatenate([u1, out_arr], axis_no)
+            out_arr = jnp.where(newest & next_value == 0, x_next, taken_in)
+            next_value = 2 * next_value
+        return out_arr
+
     tensor_rank = lax.axis_index("tensor")
     total_rows = hidden.shape[0]
     head_local = query_weight.shape[1] // HD
@@ -74,7 +86,7 @@
         lax.all_gather(kv_weight, "dp", axis=1, tiled=True),
         lax.all_gather(out_pruned, "dp", axis=1, tiled=True),
     )
-    whole = lax.all_gather(hidden, "tensor", axis=1, tiled=True)
+    whole = _choose_tracks(hidden, "tensor", 1)
     rows_float = whole.astype(jnp.float32)
     mean_square = jnp.mean(rows_float * rows_float, axis=-1, keepdims=True)
     normed = (rows_float * lax.rsqrt(mean_square + 1e-05) * norm_gain).astype(jnp.bfloat16)

time: 644 us -> 827 us (1.28)
  waiting for transfers between devices: 469 us -> 616 us
  other arithmetic: 37.3 us -> 56.9 us
  matrix products: 53 us -> 63.8 us
    ppermute x0 -> x3, waiting for transfers between devices: none -> 290 us  [_choose_tracks(): lax.ppermute(out_arr, device_axis, [(at, at ^ next_value) for at in range...]
    all_gather x1 -> x0, waiting for transfers between devices: 107 us -> none  [on_device(): whole = lax.all_gather(hidden, 'tensor', axis=1, tiled=True)]
    all_gather x1, waiting for transfers between devices: 19.9 us -> 0.02 us  [on_device(): kv_whole = lax.all_gather(kv_piece, 'tensor', axis=1, tiled=True)]
    select_n x0 -> x2, other arithmetic: none -> 10.2 us  [_choose_tracks(): out_arr = jnp.where(newest & next_value == 0, x_next, taken_in)]
    dot_general x1, matrix products: 15.6 us -> 24.5 us  [on_device(): jnp.dot(normed, query_full, preferred_element_type=jnp.float32)]
  transfers between devices with their start and end apart: 6 -> 8, of which waited for: 5 -> 4; matrix products, arithmetic and copies ran while one was open for 22% -> 18% of each run, Pallas kernels for 0% -> 0%
where the time goes in v1:
time: 827 us; the launch traced here: 826 us
  waiting for transfers between devices  616 us (74%)
  local copies, waits for them, and re-layouts  67.4 us (8%)
  matrix products  63.8 us (8%)
  other arithmetic  56.9 us (7%)
  between operations  13.4 us (2%)
    reduce_scatter x1, waiting for transfers between devices, on_device(): mixed = lax.psum_scatter(terms, 'tensor', scatter_dimension=1, tiled=True)  326 us
    ppermute x3, waiting for transfers between devices, _choose_tracks(): lax.ppermute(out_arr, device_axis, [(at, at ^ next_value) for at in range...  290 us
    mul x4, local copies, waits for them, and re-layouts, prune(): blocks = blocks * keep.astype(weight.dtype)[:, None, :, None]  58.3 us
    dot_general x1, matrix products, on_device(): jnp.dot(normed, query_full, preferred_element_type=jnp.float32)  24.5 us
    mul x2, other arithmetic, prune(): blocks = blocks * keep.astype(weight.dtype)[:, None, :, None]  24.4 us
    dot_general x1, matrix products, on_device(): terms = jnp.dot(context, out_full, preferred_element_type=jnp.float32)  17.8 us
  transfers between devices with their start and end apart: 8, of which 4 were waited for; matrix products, arithmetic and copies ran while one was open for 18% of the time, Pallas kernels for 0%

profile of v1, /device:TPU:0, one launch (start us, length us, event | category | flops | bytes accessed | tf_op | source)
XLA Modules:
  0.0 825.6 jit_solution(17152097216322664762)
XLA Ops:
  6.5 0.0 all-gather.5.cloned.1.call-start
  6.5 3.0 collective-permute-start
  9.5 27.3 %collective-permute-done = bf16[600,1024]{1,0:T(8,128)(2,1)} collective-permute-done((bf16[600,1024]{1,0:T(8,128)(2,1)}, bf16[600,1024]{1,0:T(8,128)(2,1)}, u32[]{:S(2)}, u32[]{:S(2)}) %collective-permute-start) | collective-permute-done | bytes 1228832 | tf_op jit(solution)/shard_map/ppermute | solution.py:72
  36.8 3.5 maximum_select_fusion.2
  40.3 1.9 collective-permute-start.1
  42.2 52.8 %collective-permute-done.1 = bf16[600,2048]{1,0:T(8,128)(2,1)} collective-permute-done((bf16[600,2048]{1,0:T(8,128)(2,1)S(1)}, bf16[600,2048]{1,0:T(8,128)(2,1)}, u32[]{:S(2)}, u32[]{:S(2)}) %collective-permute-start.1) | collective-permute-done | bytes 2457632 | tf_op jit(solution)/shard_map/ppermute | solution.py:72
  95.0 6.7 maximum_select_fusion.1
  101.7 2.6 collective-permute-start.2
  104.3 0.0 all-gather.5.cloned.1.call-update
  104.3 0.0 all-gather.7.cloned.1.call-start
  104.4 0.0 copy-start.5
  104.4 210.2 %collective-permute-done.2 = bf16[600,4096]{1,0:T(8,128)(2,1)} collective-permute-done((bf16[600,4096]{1,0:T(8,128)(2,1)}, bf16[600,4096]{1,0:T(8,128)(2,1)}, u32[]{:S(2)}, u32[]{:S(2)}) %collective-permute-start.2) | collective-permute-done | bytes 4915232 | tf_op jit(solution)/shard_map/ppermute | solution.py:72
  314.6 11.8 %fusion = f32[600]{0:T(1024)S(1)} fusion(bf16[600,4096]{1,0:T(8,128)(2,1)} %maximum_select_fusion.1, bf16[600,4096]{1,0:T(8,128)(2,1)} %collective-permute-done.2, pred[]{:T(512)S(6)} %eq.35), kind=kLoop, calls=%fused_computation.4 | loop fusion | flops 58981800 | bytes 9832801 | tf_op jit(solution)/shard_map/reduce_sum | solution.py:91
  326.4 0.0 copy-start.1
  326.5 0.0 all-gather.5.cloned.1.call-done
  326.5 0.0 copy-done.5
  326.5 11.6 %fusion.27 = bf16[600,256]{1,0:T(8,128)(2,1)} fusion(bf16[256,8192]{1,0:T(8,128)(2,1)} %all-gather.5.cloned.1.call-done, f32[8192]{0:T(1024)S(1)} %copy-done.5, f32[600]{0:T(1024)S(1)} %add_rsqrt_fusion, bf16[600,4096]{1,0:T(8,128)(2,1)} %collective-permute-done.2, bf16[600,4096]{1,0:T(8,128)(2,1)} %maximum_select_fusion.1, pred[]{:T(512)S(6)} %eq.35), kind=kOutput, calls=%fused_computation.41 | convolution fusion | flops 2580633600 | bytes 14367073 | tf_op jit(solution)/shard_map/dot_general | solution.py:94
  338.1 0.0 all-gather.7.cloned.1.call-update
  338.1 0.0 all-gather.9.cloned.1.call-start
  338.2 0.0 copy-done.1
  338.2 0.1 copy.25
  338.3 6.1 mul.162
  344.4 22.6 %mul.163 = bf16[4096,1024]{1,0:T(8,128)(2,1)} reshape(bf16[64,64,16,64]{3,2,1,0:T(8,128)(2,1)} %mul.162) | data formatting | bytes 16777216 | tf_op jit(solution)/shard_map/mul | solution.py:52
  366.9 10.8 %mul.164 = bf16[4096,1024]{1,0:T(8,128)(2,1)} multiply(bf16[4096,1024]{1,0:T(8,128)(2,1)} %param.13, bf16[4096,1024]{1,0:T(8,128)(2,1)} %mul.163) | non-fusion elementwise | flops 4194304 | bytes 25165824 | tf_op jit(solution)/shard_map/mul | solution.py:52
  377.7 0.0 copy-start.2
  377.7 0.0 all-gather.9.cloned.1.call-update
  377.7 0.0 all-gather.11.cloned.1.call-start
  377.8 0.6 copy-done.2
  378.4 6.4 mul.179
  384.8 23.2 %mul.180 = bf16[1024,4096]{1,0:T(8,128)(2,1)} reshape(bf16[16,64,64,64]{3,2,1,0:T(8,128)(2,1)} %mul.179) | data formatting | bytes 16777216 | tf_op jit(solution)/shard_map/mul | solution.py:52
  408.1 13.7 %mul.181 = bf16[1024,4096]{1,0:T(8,128)(2,1)} multiply(bf16[1024,4096]{1,0:T(8,128)(2,1)} %param.16, bf16[1024,4096]{1,0:T(8,128)(2,1)} %mul.180) | non-fusion elementwise | flops 4194304 | bytes 25165824 | tf_op jit(solution)/shard_map/mul | solution.py:52
  421.7 0.0 copy-start.3
  421.7 0.0 copy-start.4
  421.7 0.0 all-gather.11.cloned.1.call-update
  421.7 0.2 reduce-scatter.2.cloned.1.call-start
  422.0 0.4 copy-done.3
  422.4 0.2 reduce-window.4
  422.6 0.1 convert_reduce_fusion
  422.7 0.0 copy-done.4
  422.7 0.1 select_reduce_fusion
  422.8 0.4 or_and_fusion
  423.2 1.1 multiply_cosine_fusion
  424.3 0.0 all-gather.7.cloned.1.call-done
  424.4 2.1 slice_bitcast_fusion
  426.5 0.6 copy.40
  427.0 1.2 copy.54
  428.3 3.0 gather_fusion
  431.3 0.0 all-gather.9.cloned.1.call-done
  431.3 24.5 %fusion.9 = f32[75,8,8,128]{3,1,2,0:T(8,128)S(1)} fusion(bf16[8192,1024]{1,0:T(8,128)(2,1)} %all-gather.9.cloned.1.call-done, f32[8192]{0:T(1024)S(1)} %copy-done.5, f32[600]{0:T(1024)S(1)} %add_rsqrt_fusion, bf16[600,4096]{1,0:T(8,128)(2,1)} %collective-permute-done.2, bf16[600,4096]{1,0:T(8,128)(2,1)} %maximum_select_fusion.1, pred[]{:T(512)S(6)} %eq.35), kind=kOutput, calls=%fused_computation.21 | convolution fusion | flops 10130227200 | bytes 29100384 | tf_op jit(solution)/shard_map/dot_general | solution.py:93
  455.8 0.6 copy.39
  456.4 1.8 fusion.42
  458.2 2.9 subtract_convert_fusion
  461.0 0.7 pad_maximum_fusion
  461.7 0.8 gather_fusion.1
  462.5 0.0 copy-start
  462.5 5.5 fusion.3
  468.0 0.0 copy-done
  468.0 4.4 fusion.13
  472.5 0.0 all-gather.11.cloned.1.call-done
  472.5 17.8 %fusion.14 = f32[600,8192]{1,0:T(8,128)} fusion(bf16[1024,8192]{1,0:T(8,128)(2,1)} %all-gather.11.cloned.1.call-done, bf16[8,75,8,128]{3,2,1,0:T(8,128)(2,1)S(1)} %fusion.13), kind=kOutput, calls=%fused_computation.25 | convolution fusion | flops 10066329600 | bytes 37666816 | tf_op jit(solution)/shard_map/dot_general | solution.py:132
  490.3 0.0 reduce-scatter.2.cloned.1.call-update
  490.4 325.8 %reduce-scatter.2.cloned.1.call-done = f32[600,1024]{1,0:T(8,128)} async-done(((f32[600,8192]{1,0:T(8,128)}), f32[600,1024]{1,0:T(8,128)}) %reduce-scatter.2.cloned.1.call-update) | async-done | bytes 2457616 | tf_op jit(solution)/shard_map/reduce_scatter | solution.py:133
  816.1 2.9 convert_element_type.60
  (10 shorter events, 0.1 us)
Async XLA Ops:
  6.5 319.9 %all-gather.5.cloned.1.call-start = ((), (), s32[]{:S(2)}) async-start(), calls=%async_computation.1 | async-start | bytes 6291456 | tf_op jit(solution)/shard_map/all_gather | solution.py:86
  6.5 30.3 %collective-permute-start = (bf16[600,1024]{1,0:T(8,128)(2,1)}, bf16[600,1024]{1,0:T(8,128)(2,1)}, u32[]{:S(2)}, u32[]{:S(2)}) collective-permute-start(bf16[600,1024]{1,0:T(8,128)(2,1)} %param.11), channel_id=1, source_target_pairs={{0,2},{2,0},{4,6},{6,4},{8,10},{10,8},{12,14},{14,12},{1,3},{3,1},... | collective-permute-start | bytes 3686408 | tf_op jit(solution)/shard_map/ppermute | solution.py:72
  40.3 54.7 %collective-permute-start.1 = (bf16[600,2048]{1,0:T(8,128)(2,1)S(1)}, bf16[600,2048]{1,0:T(8,128)(2,1)}, u32[]{:S(2)}, u32[]{:S(2)}) collective-permute-start(bf16[600,2048]{1,0:T(8,128)(2,1)S(1)} %maximum_select_fusion.2), channel_id=1, source_target_pairs={{0,4},{2,6},{4,0},{6,2},{8,12},{10,14},{12,8},{14,10},{1,5},{3,7},... | collective-permute-start | bytes 7372808 | tf_op jit(solution)/shard_map/ppermute | solution.py:72
  101.7 212.9 %collective-permute-start.2 = (bf16[600,4096]{1,0:T(8,128)(2,1)}, bf16[600,4096]{1,0:T(8,128)(2,1)}, u32[]{:S(2)}, u32[]{:S(2)}) collective-permute-start(bf16[600,4096]{1,0:T(8,128)(2,1)} %maximum_select_fusion.1), channel_id=1, source_target_pairs={{0,8},{2,10},{4,12},{6,14},{8,0},{10,2},{12,4},{14,6},{1,9},{3,11}... | collective-permute-start | bytes 14745608 | tf_op jit(solution)/shard_map/ppermute | solution.py:72
  104.3 320.0 %all-gather.7.cloned.1.call-start = ((), (), s32[]{:S(2)}) async-start(), calls=%async_computation.2 | async-start | bytes 2764800 | tf_op jit(solution)/shard_map/all_gather | solution.py:97
  104.4 222.1 %copy-start.5 = (f32[8192]{0:T(1024)S(1)}, f32[8192]{0:T(1024)}, u32[]{:S(2)}) copy-start(f32[8192]{0:T(1024)} %param.12) | copy-start | bytes 98308
  326.4 11.7 %copy-start.1 = (s32[64,16]{0,1:T(8,128)S(1)}, s32[64,16]{0,1:T(8,128)}, u32[]{:S(2)}) copy-start(s32[64,16]{0,1:T(8,128)} %param.14) | copy-start | bytes 12292
  338.1 93.2 %all-gather.9.cloned.1.call-start = ((), (), s32[]{:S(2)}) async-start(), calls=%async_computation.3 | async-start | bytes 25165824 | tf_op jit(solution)/shard_map/all_gather | solution.py:84
  377.7 0.7 copy-start.2
  377.7 94.8 %all-gather.11.cloned.1.call-start = ((), (), s32[]{:S(2)}) async-start(), calls=%async_computation.4 | async-start | bytes 25165824 | tf_op jit(solution)/shard_map/all_gather | solution.py:87
  421.7 0.7 copy-start.3
  421.7 1.0 copy-start.4
  421.7 394.4 %reduce-scatter.2.cloned.1.call-start = ((), (), s32[]{:S(2)}) async-start(), calls=%async_computation.5 | async-start | bytes 22118400 | tf_op jit(solution)/shard_map/reduce_scatter | solution.py:133
  462.5 5.5 copy-start
Sparse Core Ops, SparseCore 0:
  104.5 12.8 all-gather.4
  338.2 56.4 all-gather.6
  396.3 28.2 all-gather.8
  426.0 31.2 all-gather.10
  490.5 325.5 reduce-scatter.1
